TPU v7x, 512 devices: a whole 4x8x8 slice. The times are simulated.
512 devices in a mesh: tok: 128 (over z, y, core), rep: 4 (over x).
Axes of the slice: x: 4, y: 8, z: 8, core: 2. Of those that a mesh axis runs over, the one named last changes fastest.
Arguments:
- hidden: bfloat16 [12288, 1024], P(('tok', 'rep')), may hold values from -50 to 50
- norm_gain: bfloat16 [1024], replicated, may hold values from 0.5 to 1.5
- head_weight: bfloat16 [32128, 1024], P('tok'), may hold values from -3.75 to 3.75
- targets: int32 [12288], P(('tok', 'rep')), may hold values from 0 to 32127
- lengths: int32 [64], replicated, may hold values from 96 to 288, as said below
- padding_mask: int32 [12288], P(('tok', 'rep')), may hold values from 0 to 1, as said below
- owner_map: int32 [64], replicated, may hold values from 0 to 511, as said below
Outputs:
- logprob: float32 [12288], P(('tok', 'rep'))
- entropy: float32 [12288], P(('tok', 'rep'))
- request_table: float32 [512, 2, 2], P(('tok', 'rep'))
Inputs may be any that keep to these rules, and one draw needn't show every extreme that they name: `lengths`: lengths sum to 12288; the largest is exactly 288. `padding_mask`: the last token of every sequence is live. Each device's block of 24 tokens holds at most 18 live tokens, and the first block exactly 18. `owner_map`: each device owns at most 2 requests, and some device exactly 2.
All inputs are finite; a program needn't handle non-finite values.
Results may differ from a plain program's by a relative error of at most 0.015.
The roundings to bfloat16 on the way count: a program that leaves them out, or rounds other values in their place, can miss the bound.
Values may be sent and summed in bfloat16 or wider, within the bound.
No kernel may reach another device: no remote copies, remote signals or barrier semaphores. Data moves between devices by JAX's collectives and lax.ppermute only.
A program may use at most 64 MiB of HBM per device.

v0:
```python
import jax
import jax.numpy as jnp
import numpy as np
from jax import lax
from jax.sharding import Mesh
from jax.sharding import PartitionSpec as P

SLOTS = 2
EPSILON = 1e-06
NEG_FILL = -1e30
AXES = ("z", "y", "c", "x")
PLANE = ("z", "y")
CHIP = ("c", "x")


def slice_stats(rows, ids, vocab, vocab_ids):
    logits = lax.dot_general(
        rows, vocab, (((rows.ndim - 1,), (1,)), ((), ())), preferred_element_type=jnp.float32
    )
    row_top = jnp.max(logits, axis=-1)
    weights = jnp.exp(logits - row_top[..., None])
    row_total = jnp.sum(weights, axis=-1)
    moment = jnp.sum(weights * logits, axis=-1)
    chosen = jnp.sum(jnp.where(vocab_ids == ids[..., None], logits, 0.0), axis=-1)
    return (row_top, row_total, moment, chosen)


def gather_by_sum(block, axis):
    count = lax.axis_size(axis)
    place = lax.axis_index(axis)
    buffer = jnp.zeros((count,) + block.shape, block.dtype)
    buffer = lax.dynamic_update_slice(buffer, block[None], (place,) + (0,) * block.ndim)
    return lax.psum(buffer, axis)


def shards(hidden, norm_gain, head_weight, targets, lengths, padding_mask, owner_map):
    nz, ny, nc, nx = (lax.axis_size(a) for a in AXES)
    z, y, c, x = (lax.axis_index(a) for a in AXES)
    plane_count = nz * ny
    chip_count = nc * nx
    local_rows, width = hidden.shape
    slice_width = head_weight.shape[0]
    seq_count = lengths.shape[0]
    tok_place = (z * ny + y) * nc + c
    device_place = tok_place * nx + x
    widened = hidden.astype(jnp.float32)
    mean_square = jnp.mean(widened * widened, axis=1)
    normed = (
        widened * lax.rsqrt(mean_square + EPSILON)[:, None] * norm_gain.astype(jnp.float32)[None, :]
    ).astype(jnp.bfloat16)
    state_norm = jnp.sqrt(mean_square)
    live_row = padding_mask == 1
    other_head = lax.ppermute(head_weight, "c", [(i, (i + 1) % nc) for i in range(nc)])
    other_place = (z * ny + y) * nc + (c + nc - 1) % nc
    vocab = jnp.concatenate([head_weight, other_head], axis=0)
    vocab_ids = jnp.concatenate(
        [
            tok_place * slice_width + jnp.arange(slice_width, dtype=jnp.int32),
            other_place * slice_width + jnp.arange(slice_width, dtype=jnp.int32),
        ]
    )
    meta = jnp.zeros((width,), jnp.float32)
    meta = meta.at[0:local_rows].set((targets // 256).astype(jnp.float32))
    meta = meta.at[local_rows : 2 * local_rows].set((targets % 256).astype(jnp.float32))
    meta = meta.at[2 * local_rows : 3 * local_rows].set(live_row.astype(jnp.float32))
    packet = jnp.concatenate([normed, meta.astype(jnp.bfloat16)[None, :]], axis=0)
    gathered = gather_by_sum(gather_by_sum(packet, "y"), "z")
    gathered = gathered.reshape(plane_count, local_rows + 1, width)
    meta_all = gathered[:, local_rows, :].astype(jnp.float32)
    piece_ids = (
        meta_all[:, 0:local_rows] * 256.0 + meta_all[:, local_rows : 2 * local_rows]
    ).astype(jnp.int32)
    piece_live = meta_all[:, 2 * local_rows : 3 * local_rows] > 0.5
    ids_full = jnp.concatenate([piece_ids, jnp.zeros((plane_count, 1), jnp.int32)], axis=1)
    top_p, total_p, moment_p, chosen_p = (
        part[:, :local_rows] for part in slice_stats(gathered, ids_full, vocab, vocab_ids)
    )
    seq_ends = jnp.cumsum(lengths)
    seq_ids = jnp.arange(seq_count, dtype=jnp.int32)
    block_of = (jnp.arange(plane_count, dtype=jnp.int32) * nc + c) * nx + x
    piece_rows = block_of[:, None] * local_rows + jnp.arange(local_rows, dtype=jnp.int32)[None, :]
    piece_seq = jnp.sum(
        (seq_ends[None, None, :] <= piece_rows[:, :, None]).astype(jnp.int32), axis=2
    )
    member = (piece_seq[:, :, None] == seq_ids[None, None, :]) & piece_live[:, :, None]
    part_max = jnp.max(jnp.where(member, top_p[:, :, None], NEG_FILL), axis=(0, 1))
    own_rows = device_place * local_rows + jnp.arange(local_rows, dtype=jnp.int32)
    part_norm = jnp.sum(
        jnp.where(own_rows[:, None] == seq_ends[None, :] - 1, state_norm[:, None], 0.0), axis=0
    )
    earlier_same = (owner_map[None, :] == owner_map[:, None]) & (
        seq_ids[None, :] < seq_ids[:, None]
    )
    slot_rank = jnp.sum(earlier_same.astype(jnp.int32), axis=1)
    device_ids = jnp.arange(plane_count * chip_count, dtype=jnp.int32)
    slot_hot = (owner_map[:, None, None] == device_ids[None, :, None]) & (
        slot_rank[:, None, None] == jnp.arange(SLOTS, dtype=jnp.int32)[None, None, :]
    )
    req_max = jnp.max(jnp.where(slot_hot, part_max[:, None, None], NEG_FILL), axis=0)
    req_norm = jnp.sum(jnp.where(slot_hot, part_norm[:, None, None], 0.0), axis=0)
    req = jnp.stack([req_max, req_norm], axis=2).reshape(plane_count, chip_count * SLOTS * 2)
    stats = jnp.stack([top_p, total_p, moment_p, chosen_p], axis=2).reshape(
        plane_count, local_rows * 4
    )
    outgoing = jnp.concatenate([stats, req], axis=1)
    incoming = lax.all_to_all(outgoing, PLANE, 0, 0, tiled=True)
    in_stats = incoming[:, : local_rows * 4].reshape(plane_count, local_rows, 4)
    tops = in_stats[:, :, 0]
    row_top = jnp.max(tops, axis=0)
    scale = jnp.exp(tops - row_top[None, :])
    row_total = jnp.sum(in_stats[:, :, 1] * scale, axis=0)
    row_moment = jnp.sum(in_stats[:, :, 2] * scale, axis=0)
    row_chosen = jnp.sum(in_stats[:, :, 3], axis=0)
    log_total = jnp.log(row_total)
    logprob = jnp.where(live_row, row_chosen - row_top - log_total, 0.0)
    entropy = jnp.where(live_row, row_top + log_total - row_moment / row_total, 0.0)
    in_req = incoming[:, local_rows * 4 :].reshape(plane_count, chip_count, SLOTS, 2)
    chip_max = jnp.max(in_req[..., 0], axis=0)
    chip_norm = jnp.sum(in_req[..., 1], axis=0)
    chip_pair = jnp.stack([chip_max, chip_norm], axis=2)
    got = lax.all_to_all(chip_pair, CHIP, 0, 0, tiled=True)
    final_max = jnp.max(got[..., 0], axis=0)
    final_norm = jnp.sum(got[..., 1], axis=0)
    has_slot = jnp.any(slot_hot[:, device_place, :], axis=0)
    request_table = jnp.where(has_slot[:, None], jnp.stack([final_max, final_norm], axis=1), 0.0)
    return (logprob, entropy, request_table[None])


def solution(mesh):
    tok_count, rep_count = mesh.devices.shape
    cores = 2
    side = int(round((tok_count // cores) ** 0.5))
    fine = Mesh(
        np.asarray(mesh.devices).reshape(side, tok_count // cores // side, cores, rep_count), AXES
    )
    tokens = P(AXES)
    return jax.shard_map(
        shards,
        mesh=fine,
        in_specs=(P(AXES, None), P(), P(("z", "y", "c"), None), tokens, P(), tokens, P()),
        out_specs=(tokens, tokens, P(AXES, None, None)),
        check_vma=False,
    )
```

profile of v0, /device:TPU:1, one launch (start us, length us, event | category | flops | bytes accessed | tf_op | source)
XLA Modules:
  0.0 252.8 jit_solution(15617818416284887751)
XLA Ops:
  7.2 0.7 fusion.13
  7.9 0.7 fusion.12
  8.6 0.7 constant_dynamic-update-slice_fusion
  9.4 0.7 convert_element_type.37
  10.1 0.9 fusion.6
  11.0 0.9 fusion.8
  11.9 0.1 copy.38
  12.0 2.1 dynamic_update_slice.8
  14.1 0.7 copy-done.1
  15.0 79.2 %all-reduce.5.cloned.1.call-done = bf16[1,8,25,1024]{3,1,0,2:T(8,128)(2,1)} async-done(((bf16[1,8,25,1024]{3,1,0,2:T(8,128)(2,1)}), bf16[1,8,25,1024]{3,1,0,2:T(8,128)(2,1)}) %all-reduce.5.cloned.1.call-update) | async-done | bytes 409616 | tf_op jit(solution)/shard_map/psum | solution.py:33
  94.2 0.4 broadcast_in_dim.109
  94.6 0.6 copy-done.2
  95.2 1.7 copy-done
  97.0 7.4 %collective-permute-start = (bf16[251,1024]{1,0:T(8,128)(2,1)}, bf16[251,1024]{1,0:T(8,128)(2,1)}, u32[]{:S(2)}, u32[]{:S(2)}) collective-permute-start(bf16[251,1024]{1,0:T(8,128)(2,1)} %param.15), channel_id=1, source_target_pairs={{0,4},{4,0},{1,5},{5,1},{2,6},{6,2},{3,7},{7,3},{8,12},{12,8},{9,1... | collective-permute-start | bytes 1542152 | tf_op jit(solution)/shard_map/ppermute | solution.py:53
  104.4 0.1 copy.40
  104.5 0.1 reduce-window.7
  104.6 0.1 reduce.13
  104.8 0.2 convert_reduce_fusion.1
  105.0 0.1 select_reduce_fusion.4
  105.2 1.4 convert_reduce_fusion
  106.6 0.1 iota_compare_fusion.1
  106.7 93.2 %all-reduce.7.cloned.1.call-done = bf16[64,25,1024]{2,0,1:T(8,128)(2,1)} async-done(((bf16[64,25,1024]{2,0,1:T(8,128)(2,1)}), bf16[64,25,1024]{2,0,1:T(8,128)(2,1)}) %all-reduce.7.cloned.1.call-update) | async-done | bytes 3276816 | tf_op jit(solution)/shard_map/psum | solution.py:33
  199.9 0.9 fusion.5
  200.8 0.1 slice_compare_fusion
  201.0 4.2 %fusion.16 = (f32[64,25]{0,1:T(8,128)S(1)}, f32[64,25,502]{2,0,1:T(8,128)S(1)}) fusion(bf16[64,25,1024]{2,0,1:T(8,128)(2,1)} %all-reduce.7.cloned.1.call-done, bf16[251,1024]{1,0:T(8,128)(2,1)} %collective-permute-done, bf16[251,1024]{1,0:T(8,128)(2,1)} %param.15), kind=kOutput, calls=%fused_computation.71 | convolution fusion | flops 1647811328 | bytes 7524096 | tf_op jit(solution)/shard_map/dot_general | solution.py:17
  205.2 0.1 copy.41
  205.3 0.9 select_reduce_fusion.1
  206.2 0.1 select_reduce_fusion.3
  206.3 1.0 copy.42
  207.4 1.7 reshape.263
  209.3 1.9 fusion
  211.3 0.7 copy.44
  211.9 9.8 %all-to-all-start = ((f32[64,1,128]{2,1,0:T(1,128)}), f32[64,1,128]{2,1,0:T(1,128)S(1)}, u32[]{:S(2)}, u32[]{:S(2)}) async-start(f32[64,1,128]{2,1,0:T(1,128)} %copy.44), calls=%async_computation | async-start | bytes 65536 | tf_op jit(solution)/shard_map/all_to_all | solution.py:106
  221.8 0.1 broadcast_and_fusion
  221.9 0.2 dynamic-slice_reduce_fusion
  222.1 10.5 %all-to-all-done = f32[64,1,128]{2,1,0:T(1,128)S(1)} async-done(((f32[64,1,128]{2,1,0:T(1,128)}), f32[64,1,128]{2,1,0:T(1,128)S(1)}, u32[]{:S(2)}, u32[]{:S(2)}) %all-to-all-start) | async-done | bytes 32800 | tf_op jit(solution)/shard_map/all_to_all | solution.py:106
  232.6 0.1 copy.45
  232.7 0.3 fusion.15
  233.0 0.1 slice_reduce_fusion.2
  233.1 0.1 copy.49
  233.2 0.1 copy.48
  233.3 0.7 copy.50
  234.0 6.4 %all-to-all-start.1 = ((f32[8,2,2]{1,2,0:T(2,128)}), f32[8,2,2]{1,2,0:T(2,128)S(1)}, u32[]{:S(2)}, u32[]{:S(2)}) async-start(f32[8,2,2]{1,2,0:T(2,128)} %copy.50), calls=%async_computation.1 | async-start | bytes 16384 | tf_op jit(solution)/shard_map/all_to_all | solution.py:121
  240.4 0.1 reduce_max.57
  240.5 0.2 multiply_reduce_fusion.1
  240.7 0.5 subtract_select_fusion
  241.2 4.0 %all-to-all-done.1 = f32[8,2,2]{1,2,0:T(2,128)S(1)} async-done(((f32[8,2,2]{1,2,0:T(2,128)}), f32[8,2,2]{1,2,0:T(2,128)S(1)}, u32[]{:S(2)}, u32[]{:S(2)}) %all-to-all-start.1) | async-done | bytes 160 | tf_op jit(solution)/shard_map/all_to_all | solution.py:121
  245.3 0.7 copy.51
  (44 shorter events, 0.8 us)
Async XLA Ops:
  7.2 87.0 %all-reduce.5.cloned.1.call-start = ((), (), s32[]{:S(2)}) async-start(), calls=%async_computation.2 | async-start | bytes 819200 | tf_op jit(solution)/shard_map/psum | solution.py:33
  14.1 0.8 copy-start.1
  14.9 185.0 %all-reduce.7.cloned.1.call-start = ((), (), s32[]{:S(2)}) async-start(), calls=%async_computation.3 | async-start | bytes 6553600 | tf_op jit(solution)/shard_map/psum | solution.py:33
  15.0 89.4 %copy-start.3 = (s32[64]{0:T(128)S(1)}, s32[64]{0:T(128)}, u32[]{:S(2)}) copy-start(s32[64]{0:T(128)} %param.17) | copy-start | bytes 772
  15.0 89.9 %copy-start.4 = (s32[64]{0:T(128)S(1)}, s32[64]{0:T(128)}, u32[]{:S(2)}) copy-start(s32[64]{0:T(128)} %param.19) | copy-start | bytes 772
  94.2 1.0 copy-start.2
  95.2 1.7 copy-start
  97.0 104.0 %collective-permute-start = (bf16[251,1024]{1,0:T(8,128)(2,1)}, bf16[251,1024]{1,0:T(8,128)(2,1)}, u32[]{:S(2)}, u32[]{:S(2)}) collective-permute-start(bf16[251,1024]{1,0:T(8,128)(2,1)} %param.15), channel_id=1, source_target_pairs={{0,4},{4,0},{1,5},{5,1},{2,6},{6,2},{3,7},{7,3},{8,12},{12,8},{9,1... | collective-permute-start | bytes 1542152 | tf_op jit(solution)/shard_map/ppermute | solution.py:53
  205.2 35.5 %copy-start.5 = (s32[24]{0:T(128)S(1)}, s32[24]{0:T(128)}, u32[]{:S(2)}) copy-start(s32[24]{0:T(128)} %param.18) | copy-start | bytes 292
  211.9 20.7 %all-to-all-start = ((f32[64,1,128]{2,1,0:T(1,128)}), f32[64,1,128]{2,1,0:T(1,128)S(1)}, u32[]{:S(2)}, u32[]{:S(2)}) async-start(f32[64,1,128]{2,1,0:T(1,128)} %copy.44), calls=%async_computation | async-start | bytes 65536 | tf_op jit(solution)/shard_map/all_to_all | solution.py:106
  234.0 11.3 %all-to-all-start.1 = ((f32[8,2,2]{1,2,0:T(2,128)}), f32[8,2,2]{1,2,0:T(2,128)S(1)}, u32[]{:S(2)}, u32[]{:S(2)}) async-start(f32[8,2,2]{1,2,0:T(2,128)} %copy.50), calls=%async_computation.1 | async-start | bytes 16384 | tf_op jit(solution)/shard_map/all_to_all | solution.py:121
Sparse Core Ops, SparseCore 0:
  15.0 79.1 all-reduce.4
  97.1 102.7 all-reduce.6
where the time goes:
time: 253 us
  waiting for transfers between devices  187 us (74%)
  starting transfers between devices  23.7 us (9%)
  between operations  14.4 us (6%)
  other arithmetic  12.4 us (5%)
  local copies, waits for them, and re-layouts  11.1 us (4%)
  matrix products  4.21 us (2%)
    psum x2, waiting for transfers between devices, gather_by_sum(): return lax.psum(buffer, axis)  172 us
    all_to_all x1, waiting for transfers between devices, shards(): incoming = lax.all_to_all(outgoing, PLANE, 0, 0, tiled=True)  10.5 us
    all_to_all x1, starting transfers between devices, shards(): incoming = lax.all_to_all(outgoing, PLANE, 0, 0, tiled=True)  9.85 us
    ppermute x1, starting transfers between devices, shards(): lax.ppermute(head_weight, 'c', [(i, (i + 1) % nc) for i in range(nc)])  7.37 us
    all_to_all x1, starting transfers between devices, shards(): got = lax.all_to_all(chip_pair, CHIP, 0, 0, tiled=True)  6.39 us
  transfers between devices with their start and end apart: 5, of which 4 were waited for; matrix products, arithmetic and copies ran while one was open for 2% of the time, Pallas kernels for 0%

commit v1 on v0

--- a/solution.py
+++ b/solution.py
@@ -30,7 +30,7 @@
     place = lax.axis_index(axis)
     buffer = jnp.zeros((count,) + block.shape, block.dtype)
     buffer = lax.dynamic_update_slice(buffer, block[None], (place,) + (0,) * block.ndim)
-    return lax.psum(buffer, axis)
+    return jnp.sum(lax.all_gather(buffer, axis_name=axis), axis=0)
 
 
 def shards(hidden, norm_gain, head_weight, targets, lengths, padding_mask, owner_map):

time: 253 us -> 400 us (1.58)
  waiting for transfers between devices: 187 us -> 325 us
  other arithmetic: 12.4 us -> 27.8 us
  starting transfers between devices: 23.7 us -> 18.9 us
    all_gather x0 -> x2, waiting for transfers between devices: none -> 311 us  [gather_by_sum(): return jnp.sum(lax.all_gather(buffer, axis_name=axis), axis=0)]
    psum x2 -> x0, waiting for transfers between devices: 172 us -> none  [gather_by_sum(): return lax.psum(buffer, axis)]
    reduce_sum x0 -> x2, other arithmetic: none -> 13.5 us  [gather_by_sum(): return jnp.sum(lax.all_gather(buffer, axis_name=axis), axis=0)]
    ppermute x1, starting transfers between devices: 7.37 us -> 2.64 us  [shards(): lax.ppermute(head_weight, 'c', [(i, (i + 1) % nc) for i in range(nc)])]
  transfers between devices with their start and end apart: 5 -> 5, of which waited for: 4 -> 4; matrix products, arithmetic and copies ran while one was open for 2% -> 4% of each run, Pallas kernels for 0% -> 0%
where the time goes in v1:
time: 400 us
  waiting for transfers between devices  325 us (81%)
  other arithmetic  27.8 us (7%)
  starting transfers between devices  18.9 us (5%)
  between operations  14.4 us (4%)
  local copies, waits for them, and re-layouts  10.4 us (3%)
    all_gather x2, waiting for transfers between devices, gather_by_sum(): return jnp.sum(lax.all_gather(buffer, axis_name=axis), axis=0)  311 us
    reduce_sum x2, other arithmetic, gather_by_sum(): return jnp.sum(lax.all_gather(buffer, axis_name=axis), axis=0)  13.5 us
    all_to_all x1, waiting for transfers between devices, shards(): incoming = lax.all_to_all(outgoing, PLANE, 0, 0, tiled=True)  10.5 us
    all_to_all x1, starting transfers between devices, shards(): incoming = lax.all_to_all(outgoing, PLANE, 0, 0, tiled=True)  9.8 us
  transfers between devices with their start and end apart: 5, of which 4 were waited for; matrix products, arithmetic and copies ran while one was open for 4% of the time, Pallas kernels for 0%

profile of v1, /device:TPU:1, one launch (start us, length us, event | category | flops | bytes accessed | tf_op | source)
XLA Modules:
  0.0 399.9 jit_solution(13910792004376625661)
XLA Ops:
  7.2 0.9 fusion.6
  8.1 0.7 convert_element_type.41
  8.8 0.7 fusion.13
  9.5 0.7 fusion.12
  10.2 0.7 constant_dynamic-update-slice_fusion
  11.0 0.9 fusion.8
  12.0 2.1 dynamic_update_slice.8
  14.1 0.7 copy-done.1
  15.0 54.1 %all-gather.3.cloned.1.call-done = bf16[8,8,25,1024]{3,1,2,0:T(8,128)(2,1)} async-done(((bf16[1,8,25,1024]{3,1,2,0:T(8,128)(2,1)}), bf16[8,8,25,1024]{3,1,2,0:T(8,128)(2,1)}) %all-gather.3.cloned.1.call-update) | async-done | bytes 3276816 | tf_op jit(solution)/shard_map/all_gather | solution.py:33
  69.0 3.4 reduce_sum.142
  72.5 0.4 broadcast_in_dim.65
  72.9 0.6 copy-done.2
  73.5 1.7 copy-done
  75.2 2.6 collective-permute-start
  77.9 0.1 copy.78
  78.0 0.1 reduce-window.7
  78.1 0.1 reduce.15
  78.3 0.2 convert_reduce_fusion.1
  78.5 0.6 select_reduce_fusion.4
  79.2 2.0 convert_reduce_fusion
  81.2 0.5 iota_compare_fusion.3
  81.7 0.7 iota_compare_fusion.1
  82.4 256.7 %all-gather.5.cloned.1.call-done = bf16[8,8,8,25,1024]{4,2,3,1,0:T(8,128)(2,1)} async-done(((bf16[1,8,8,25,1024]{4,2,3,1,0:T(8,128)(2,1)}), bf16[8,8,8,25,1024]{4,2,3,1,0:T(8,128)(2,1)}) %all-gather.5.cloned.1.call-update) | async-done | bytes 26214416 | tf_op jit(solution)/shard_map/all_gather | solution.py:33
  339.1 10.0 %reduce_sum.143 = bf16[8,8,25,1024]{3,1,2,0:T(8,128)(2,1)S(1)} reduce(bf16[8,8,8,25,1024]{4,2,3,1,0:T(8,128)(2,1)} %all-gather.5.cloned.1.call-done, bf16[]{:T(256)} %constant.149.clone.1), dimensions={0}, to_apply=%region_2.3 | reduce | flops 11468800 | bytes 29491202 | tf_op jit(solution)/shard_map/reduce_sum | solution.py:33
  349.2 0.4 copy.97
  349.6 0.7 fusion.9
  350.3 0.8 copy.92
  351.2 3.2 fusion.16
  354.5 1.9 fusion
  356.5 0.9 select_reduce_fusion.1
  357.4 0.1 select_reduce_fusion.3
  357.6 0.3 copy.80
  357.8 0.7 reshape.269
  358.7 0.7 copy.82
  359.4 9.8 %all-to-all-start = ((f32[64,1,128]{2,1,0:T(1,128)}), f32[64,1,128]{2,1,0:T(1,128)S(1)}, u32[]{:S(2)}, u32[]{:S(2)}) async-start(f32[64,1,128]{2,1,0:T(1,128)} %copy.82), calls=%async_computation | async-start | bytes 65536 | tf_op jit(solution)/shard_map/all_to_all | solution.py:106
  369.2 0.1 broadcast_and_fusion
  369.3 0.2 dynamic-slice_reduce_fusion
  369.5 10.5 %all-to-all-done = f32[64,1,128]{2,1,0:T(1,128)S(1)} async-done(((f32[64,1,128]{2,1,0:T(1,128)}), f32[64,1,128]{2,1,0:T(1,128)S(1)}, u32[]{:S(2)}, u32[]{:S(2)}) %all-to-all-start) | async-done | bytes 32800 | tf_op jit(solution)/shard_map/all_to_all | solution.py:106
  380.0 0.1 copy.83
  380.1 0.1 slice_reduce_fusion.2
  380.4 0.7 copy.88
  381.1 6.4 %all-to-all-start.1 = ((f32[8,2,2]{1,2,0:T(2,128)}), f32[8,2,2]{1,2,0:T(2,128)S(1)}, u32[]{:S(2)}, u32[]{:S(2)}) async-start(f32[8,2,2]{1,2,0:T(2,128)} %copy.88), calls=%async_computation.1 | async-start | bytes 16384 | tf_op jit(solution)/shard_map/all_to_all | solution.py:121
  387.5 0.3 fusion.15
  387.8 0.1 reduce_max.57
  387.9 0.2 multiply_reduce_fusion.1
  388.1 0.5 subtract_select_fusion
  388.6 3.8 all-to-all-done.1
  392.4 0.7 copy.89
  (55 shorter events, 1.1 us)
Async XLA Ops:
  7.2 61.9 %all-gather.3.cloned.1.call-start = ((), (), s32[]{:S(2)}) async-start(), calls=%async_computation.2 | async-start | bytes 3686400 | tf_op jit(solution)/shard_map/all_gather | solution.py:33
  14.1 0.8 copy-start.1
  14.9 324.2 %all-gather.5.cloned.1.call-start = ((), (), s32[]{:S(2)}) async-start(), calls=%async_computation.3 | async-start | bytes 29491200 | tf_op jit(solution)/shard_map/all_gather | solution.py:33
  72.5 1.0 copy-start.2
  72.5 5.4 %copy-start.7 = (s32[64]{0:T(128)S(1)}, s32[64]{0:T(128)}, u32[]{:S(2)}) copy-start(s32[64]{0:T(128)} %param.17) | copy-start | bytes 772
  72.5 5.9 %copy-start.8 = (s32[64]{0:T(128)S(1)}, s32[64]{0:T(128)}, u32[]{:S(2)}) copy-start(s32[64]{0:T(128)} %param.19) | copy-start | bytes 772
  73.5 1.7 copy-start
  75.2 276.0 %collective-permute-start = (bf16[251,1024]{1,0:T(8,128)(2,1)}, bf16[251,1024]{1,0:T(8,128)(2,1)}, u32[]{:S(2)}, u32[]{:S(2)}) collective-permute-start(bf16[251,1024]{1,0:T(8,128)(2,1)} %param.15), channel_id=1, source_target_pairs={{0,4},{4,0},{1,5},{5,1},{2,6},{6,2},{3,7},{7,3},{8,12},{12,8},{9,1... | collective-permute-start | bytes 1542152 | tf_op jit(solution)/shard_map/ppermute | solution.py:53
  354.4 2.1 copy-start.4
  354.4 2.9 copy-start.3
  354.4 2.9 copy-start.5
  354.4 2.9 copy-start.6
  354.5 33.6 %copy-start.9 = (s32[24]{0:T(128)S(1)}, s32[24]{0:T(128)}, u32[]{:S(2)}) copy-start(s32[24]{0:T(128)} %param.18) | copy-start | bytes 292
  359.4 20.6 %all-to-all-start = ((f32[64,1,128]{2,1,0:T(1,128)}), f32[64,1,128]{2,1,0:T(1,128)S(1)}, u32[]{:S(2)}, u32[]{:S(2)}) async-start(f32[64,1,128]{2,1,0:T(1,128)} %copy.82), calls=%async_computation | async-start | bytes 65536 | tf_op jit(solution)/shard_map/all_to_all | solution.py:106
  381.1 11.3 %all-to-all-start.1 = ((f32[8,2,2]{1,2,0:T(2,128)}), f32[8,2,2]{1,2,0:T(2,128)S(1)}, u32[]{:S(2)}, u32[]{:S(2)}) async-start(f32[8,2,2]{1,2,0:T(2,128)} %copy.88), calls=%async_computation.1 | async-start | bytes 16384 | tf_op jit(solution)/shard_map/all_to_all | solution.py:121
Sparse Core Ops, SparseCore 0:
  15.0 53.9 all-gather.2
  75.3 263.7 all-gather.4
